TPU v7x, 32 devices: a whole 2x2x4 slice. The times are simulated.
32 devices in a mesh: dp: 8 (over y, x, core), ctx: 4 (over z).
Axes of the slice: x: 2, y: 2, z: 4, core: 2. Of those that a mesh axis runs over, the one named last changes fastest.
Arguments:
- inputs: bfloat16 [16, 1024, 768], P('dp', 'ctx'), may hold values from -6 to 6
- lengths: int32 [16], P('dp'), may hold values from 921 to 1024, as said below
- ln1_gain: bfloat16 [768], P(('dp', 'ctx')), may hold values from 0.5 to 1.5
- ln1_bias: bfloat16 [768], P(('dp', 'ctx')), may hold values from -4 to 4
- query_weight: bfloat16 [768, 768], P(('dp', 'ctx')), may hold values from -0.3125 to 0.3125
- query_bias: bfloat16 [768], P(('dp', 'ctx')), may hold values from -4 to 4
- key_weight: bfloat16 [768, 768], P(('dp', 'ctx')), may hold values from -0.3125 to 0.3125
- value_weight: bfloat16 [768, 768], P(('dp', 'ctx')), may hold values from -0.21875 to 0.21875
- value_bias: bfloat16 [768], P(('dp', 'ctx')), may hold values from -0.75 to 0.75
- out_weight: bfloat16 [768, 768], P(('dp', 'ctx')), may hold values from -1.75 to 1.75
- out_bias: bfloat16 [768], P(('dp', 'ctx')), may hold values from -4 to 4
- ln2_gain: bfloat16 [768], P(('dp', 'ctx')), may hold values from 0.5 to 1.5
- ln2_bias: bfloat16 [768], P(('dp', 'ctx')), may hold values from -4 to 4
- ffn_in_weight: bfloat16 [768, 3072], P(('dp', 'ctx')), may hold values from -0.21875 to 0.21875
- ffn_in_bias: bfloat16 [3072], P(('dp', 'ctx')), may hold values from -4 to 4
- ffn_out_weight: bfloat16 [3072, 768], P(('dp', 'ctx')), may hold values from -0.15625 to 0.15625
- ffn_out_bias: bfloat16 [768], P(('dp', 'ctx')), may hold values from -4 to 4
- out_grad: bfloat16 [16, 1024, 768], P('dp', 'ctx'), may hold values from -6 to 6
Outputs:
- output: bfloat16 [16, 1024, 768], P('dp', 'ctx')
- input_grad: bfloat16 [16, 1024, 768], P('dp', 'ctx')
- grad_ln1_gain: float32 [768], P(('dp', 'ctx'))
- grad_ln1_bias: float32 [768], P(('dp', 'ctx'))
- grad_query: float32 [768, 768], P(('dp', 'ctx'))
- grad_query_bias: float32 [768], P(('dp', 'ctx'))
- grad_key: float32 [768, 768], P(('dp', 'ctx'))
- grad_value: float32 [768, 768], P(('dp', 'ctx'))
- grad_value_bias: float32 [768], P(('dp', 'ctx'))
- grad_out: float32 [768, 768], P(('dp', 'ctx'))
- grad_out_bias: float32 [768], P(('dp', 'ctx'))
- grad_ln2_gain: float32 [768], P(('dp', 'ctx'))
- grad_ln2_bias: float32 [768], P(('dp', 'ctx'))
- grad_ffn_in: float32 [768, 3072], P(('dp', 'ctx'))
- grad_ffn_in_bias: float32 [3072], P(('dp', 'ctx'))
- grad_ffn_out: float32 [3072, 768], P(('dp', 'ctx'))
- grad_ffn_out_bias: float32 [768], P(('dp', 'ctx'))
Inputs may be any that keep to these rules, and one draw needn't show every extreme that they name: `lengths`: A sequence's molecules occupy positions 0 to its length - 1; some sequence has exactly 1024, some exactly 921.
All inputs are finite; a program needn't handle non-finite values.
Results may differ from a plain program's by a relative error of at most 0.015.
Values may be sent and summed in bfloat16 or wider, within the bound.
No kernel may reach another device: no remote copies, remote signals or barrier semaphores. Data moves between devices by JAX's collectives and lax.ppermute only.
A program may use at most 192 MiB of HBM per device.

v0:
```python
import jax
import jax.numpy as jnp
from jax import lax
from jax.sharding import PartitionSpec as P

H = 12
HD = 64


def layer_norm(tok_rows, gain, shift):
    center = tok_rows - jnp.mean(tok_rows, axis=-1, keepdims=True)
    spread = jnp.mean(center * center, axis=-1, keepdims=True)
    return center * lax.rsqrt(spread + 1e-06) * gain + shift


def gelu_exact(values):
    return jax.nn.gelu(values, approximate=False)


def outer_product(left_rows, right_rows):
    return lax.dot_general(
        left_rows, right_rows, (((0,), (0,)), ((), ())), preferred_element_type=jnp.float32
    )


def back_product(grad_rows, weight):
    return lax.dot_general(
        grad_rows, weight, (((1,), (1,)), ((), ())), preferred_element_type=jnp.float32
    )


def column_sum(grad_rows):
    return jnp.sum(grad_rows.astype(jnp.float32), axis=0)


def fetch(shards):
    return (
        lax.all_gather(shards[0], ("dp", "ctx"), axis=0, tiled=True),
        lax.all_gather(shards[1], ("dp", "ctx"), axis=0, tiled=True),
        lax.all_gather(shards[2], ("dp", "ctx"), axis=0, tiled=True),
        lax.all_gather(shards[3], ("dp", "ctx"), axis=0, tiled=True),
        lax.all_gather(shards[4], ("dp", "ctx"), axis=0, tiled=True),
        lax.all_gather(shards[5], ("dp", "ctx"), axis=0, tiled=True),
        lax.all_gather(shards[6], ("dp", "ctx"), axis=0, tiled=True),
        lax.all_gather(shards[7], ("dp", "ctx"), axis=0, tiled=True),
        lax.all_gather(shards[8], ("dp", "ctx"), axis=0, tiled=True),
        lax.all_gather(shards[9], ("dp", "ctx"), axis=0, tiled=True),
        lax.all_gather(shards[10], ("dp", "ctx"), axis=0, tiled=True),
        lax.all_gather(shards[11], ("dp", "ctx"), axis=0, tiled=True),
        lax.all_gather(shards[12], ("dp", "ctx"), axis=0, tiled=True),
        lax.all_gather(shards[13], ("dp", "ctx"), axis=0, tiled=True),
        lax.all_gather(shards[14], ("dp", "ctx"), axis=0, tiled=True),
    )


def forward(tok_block, length, full_set):
    (
        ln1_gain,
        ln1_bias,
        query_weight,
        query_bias,
        key_weight,
        value_weight,
        value_bias,
        out_weight,
        out_bias,
        ln2_gain,
        ln2_bias,
        ffn_in_weight,
        ffn_in_bias,
        ffn_out_weight,
        ffn_out_bias,
    ) = full_set
    seq_rows = tok_block.shape[0]
    tok_rows = tok_block.astype(jnp.float32)
    normed = layer_norm(
        tok_rows, ln1_gain.astype(jnp.float32), ln1_bias.astype(jnp.float32)
    ).astype(jnp.bfloat16)
    queries = (
        jnp.dot(normed, query_weight, preferred_element_type=jnp.float32)
        + query_bias.astype(jnp.float32)
    ).astype(jnp.bfloat16)
    key_rows = jnp.dot(normed, key_weight, preferred_element_type=jnp.float32).astype(jnp.bfloat16)
    value_rows = (
        jnp.dot(normed, value_weight, preferred_element_type=jnp.float32)
        + value_bias.astype(jnp.float32)
    ).astype(jnp.bfloat16)
    all_keys, all_values = (
        lax.all_gather(key_rows, "ctx", axis=0, tiled=True),
        lax.all_gather(value_rows, "ctx", axis=0, tiled=True),
    )
    total_rows = all_keys.shape[0]
    query_heads = queries.reshape(seq_rows, H, HD)
    key_heads = all_keys.reshape(total_rows, H, HD)
    value_heads = all_values.reshape(total_rows, H, HD)
    scores = jnp.einsum(
        "qhd,khd->hqk", query_heads, key_heads, preferred_element_type=jnp.float32
    ) * HD ** (-0.5)
    valid = jnp.arange(total_rows) < length
    scores = jnp.where(valid[None, None, :], scores, -1e30)
    log_total = jax.nn.logsumexp(scores, axis=-1)
    attn_probs = jax.nn.softmax(scores, axis=-1)
    low_probs = attn_probs.astype(jnp.bfloat16)
    mixed_rows = jnp.einsum(
        "hqk,khd->qhd", low_probs, value_heads, preferred_element_type=jnp.float32
    )
    mixed_rows = mixed_rows.reshape(seq_rows, H * HD).astype(jnp.bfloat16)
    middle = (
        tok_rows
        + jnp.dot(mixed_rows, out_weight, preferred_element_type=jnp.float32)
        + out_bias.astype(jnp.float32)
    )
    normed_two = layer_norm(
        middle, ln2_gain.astype(jnp.float32), ln2_bias.astype(jnp.float32)
    ).astype(jnp.bfloat16)
    ffn_pre = jnp.dot(
        normed_two, ffn_in_weight, preferred_element_type=jnp.float32
    ) + ffn_in_bias.astype(jnp.float32)
    ffn_act = gelu_exact(ffn_pre).astype(jnp.bfloat16)
    result = (
        middle
        + jnp.dot(ffn_act, ffn_out_weight, preferred_element_type=jnp.float32)
        + ffn_out_bias.astype(jnp.float32)
    )
    kept = (
        tok_rows,
        normed,
        query_heads,
        key_heads,
        value_heads,
        attn_probs,
        low_probs,
        mixed_rows,
        middle,
        normed_two,
        ffn_pre,
        ffn_act,
        log_total,
        length,
    )
    return (result.astype(jnp.bfloat16), kept)


def backward(kept, cot_block, full_set):
    (
        ln1_gain,
        ln1_bias,
        query_weight,
        query_bias,
        key_weight,
        value_weight,
        value_bias,
        out_weight,
        out_bias,
        ln2_gain,
        ln2_bias,
        ffn_in_weight,
        ffn_in_bias,
        ffn_out_weight,
        ffn_out_bias,
    ) = full_set
    (
        tok_rows,
        normed,
        query_heads,
        key_heads,
        value_heads,
        attn_probs,
        low_probs,
        mixed_rows,
        middle,
        normed_two,
        ffn_pre,
        ffn_act,
        log_total,
        length,
    ) = kept
    seq_rows = tok_rows.shape[0]
    total_rows = key_heads.shape[0]
    score_scale = HD ** (-0.5)
    d_out = cot_block.astype(jnp.float32)
    d_ffn_out = d_out.astype(jnp.bfloat16)
    grad_ffn_out_bias = column_sum(d_ffn_out)
    grad_ffn_out = outer_product(ffn_act, d_ffn_out)
    d_act = back_product(d_ffn_out, ffn_out_weight)
    unused, gelu_back = jax.vjp(gelu_exact, ffn_pre)
    d_pre = gelu_back(d_act)[0].astype(jnp.bfloat16)
    grad_ffn_in_bias = column_sum(d_pre)
    grad_ffn_in = outer_product(normed_two, d_pre)
    d_normed_two = back_product(d_pre, ffn_in_weight)
    unused, second_back = jax.vjp(
        layer_norm, middle, ln2_gain.astype(jnp.float32), ln2_bias.astype(jnp.float32)
    )
    d_middle, grad_ln2_gain, grad_ln2_bias = second_back(d_normed_two)
    d_middle = d_middle + d_out
    d_branch = d_middle.astype(jnp.bfloat16)
    grad_out_bias = column_sum(d_branch)
    grad_out = outer_product(mixed_rows, d_branch)
    d_mixed = back_product(d_branch, out_weight).astype(jnp.bfloat16).reshape(seq_rows, H, HD)
    d_probs = jnp.einsum("qhd,khd->hqk", d_mixed, value_heads, preferred_element_type=jnp.float32)
    row_inner = jnp.sum(attn_probs * d_probs, axis=-1, keepdims=True)
    d_scores = (attn_probs * (d_probs - row_inner)).astype(jnp.bfloat16)
    d_query = (
        jnp.einsum("hqk,khd->qhd", d_scores, key_heads, preferred_element_type=jnp.float32)
        * score_scale
    )
    d_query = d_query.reshape(seq_rows, H * HD).astype(jnp.bfloat16)
    key_terms = (
        jnp.einsum("hqk,qhd->khd", d_scores, query_heads, preferred_element_type=jnp.float32)
        * score_scale
    )
    value_terms = jnp.einsum("hqk,qhd->khd", low_probs, d_mixed, preferred_element_type=jnp.float32)
    key_sums, value_sums = (
        lax.psum_scatter(
            key_terms.reshape(total_rows, H * HD).astype(jnp.bfloat16),
            "ctx",
            scatter_dimension=0,
            tiled=True,
        ).astype(jnp.float32),
        lax.psum_scatter(
            value_terms.reshape(total_rows, H * HD).astype(jnp.bfloat16),
            "ctx",
            scatter_dimension=0,
            tiled=True,
        ).astype(jnp.float32),
    )
    d_key = key_sums.astype(jnp.bfloat16)
    d_value = value_sums.astype(jnp.bfloat16)
    grad_query_bias = column_sum(d_query)
    grad_value_bias = column_sum(d_value)
    grad_query = outer_product(normed, d_query)
    grad_key = outer_product(normed, d_key)
    grad_value = outer_product(normed, d_value)
    d_normed = (
        back_product(d_query, query_weight)
        + back_product(d_key, key_weight)
        + back_product(d_value, value_weight)
    )
    unused, first_back = jax.vjp(
        layer_norm, tok_rows, ln1_gain.astype(jnp.float32), ln1_bias.astype(jnp.float32)
    )
    d_rows, grad_ln1_gain, grad_ln1_bias = first_back(d_normed)
    d_input = (d_middle + d_rows).astype(jnp.bfloat16)
    grads = (
        grad_ln1_gain,
        grad_ln1_bias,
        grad_query,
        grad_query_bias,
        grad_key,
        grad_value,
        grad_value_bias,
        grad_out,
        grad_out_bias,
        grad_ln2_gain,
        grad_ln2_bias,
        grad_ffn_in,
        grad_ffn_in_bias,
        grad_ffn_out,
        grad_ffn_out_bias,
    )
    return (d_input, grads)


def per_device(
    inputs,
    lengths,
    ln1_gain,
    ln1_bias,
    query_weight,
    query_bias,
    key_weight,
    value_weight,
    value_bias,
    out_weight,
    out_bias,
    ln2_gain,
    ln2_bias,
    ffn_in_weight,
    ffn_in_bias,
    ffn_out_weight,
    ffn_out_bias,
    out_grad,
):
    shards = (
        ln1_gain,
        ln1_bias,
        query_weight,
        query_bias,
        key_weight,
        value_weight,
        value_bias,
        out_weight,
        out_bias,
        ln2_gain,
        ln2_bias,
        ffn_in_weight,
        ffn_in_bias,
        ffn_out_weight,
        ffn_out_bias,
    )

    def forward_step(counter, seq_entry):
        tok_block, length = seq_entry
        result, kept = forward(tok_block, length, fetch(shards))
        return (counter, result)

    counter, output = lax.scan(forward_step, jnp.zeros((), jnp.int32), (inputs, lengths))

    def backward_step(totals, seq_entry):
        tok_block, length, cot_block = seq_entry
        full_set = fetch(shards)
        unused, kept = forward(tok_block, length, full_set)
        d_input, grads = backward(kept, cot_block, full_set)
        return (jax.tree.map(jnp.add, totals, grads), d_input)

    groups = lax.axis_size(("dp", "ctx"))
    start_totals = tuple(
        (
            jnp.zeros((shard_item.shape[0] * groups,) + shard_item.shape[1:], jnp.float32)
            for shard_item in shards
        )
    )
    totals, input_grad = lax.scan(backward_step, start_totals, (inputs, lengths, out_grad))
    grad_shards = lax.psum_scatter(totals, ("dp", "ctx"), scatter_dimension=0, tiled=True)
    return (output, input_grad) + tuple(grad_shards)


def solution(mesh):
    return jax.shard_map(
        per_device,
        mesh=mesh,
        in_specs=(
            P("dp", "ctx", None),
            P("dp"),
            P(("dp", "ctx")),
            P(("dp", "ctx")),
            P(("dp", "ctx"), None),
            P(("dp", "ctx")),
            P(("dp", "ctx"), None),
            P(("dp", "ctx"), None),
            P(("dp", "ctx")),
            P(("dp", "ctx"), None),
            P(("dp", "ctx")),
            P(("dp", "ctx")),
            P(("dp", "ctx")),
            P(("dp", "ctx"), None),
            P(("dp", "ctx")),
            P(("dp", "ctx"), None),
            P(("dp", "ctx")),
            P("dp", "ctx", None),
        ),
        out_specs=(
            P("dp", "ctx", None),
            P("dp", "ctx", None),
            P(("dp", "ctx")),
            P(("dp", "ctx")),
            P(("dp", "ctx"), None),
            P(("dp", "ctx")),
            P(("dp", "ctx"), None),
            P(("dp", "ctx"), None),
            P(("dp", "ctx")),
            P(("dp", "ctx"), None),
            P(("dp", "ctx")),
            P(("dp", "ctx")),
            P(("dp", "ctx")),
            P(("dp", "ctx"), None),
            P(("dp", "ctx")),
            P(("dp", "ctx"), None),
            P(("dp", "ctx")),
        ),
        check_vma=False,
    )
```

profile of v0, /device:TPU:0, one launch (start us, length us, event | category | flops | bytes accessed | tf_op | source)
XLA Modules:
  0.0 2723.2 jit_solution(3749500177245971645)
XLA Ops:
  8.2 888.4 %while.51 = (s32[]{:T(128)}, bf16[2,256,768]{2,1,0:T(8,128)(2,1)S(1)}, bf16[2,256,768]{2,1,0:T(8,128)(2,1)}, bf16[24]{0:T(256)(128)(2,1)}, bf16[24]{0:T(256)(128...) while((s32[]{:T(128)}, ...), condition=%wide.region_7.8_spmd, body=%wide.region_0.7_spmd.sunk | while | flops 4508832256 | bytes 116793320 | solution.py:307
  71.7 52.9 %all-gather.17.cloned.1.call-done = bf16[768,768]{1,0:T(8,128)(2,1)} async-done(((bf16[24,768]{1,0:T(8,128)(2,1)}), bf16[768,768]{1,0:T(8,128)(2,1)}) %all-gather.17.cloned.1.call-update) | async-done | bytes 1179664 | tf_op jit(solution)/shard_map/while/body/eval_jaxpr/all_gather | solution.py:43
  132.9 47.5 %all-gather.21.cloned.1.call-done = bf16[768,768]{1,0:T(8,128)(2,1)} async-done(((bf16[24,768]{1,0:T(8,128)(2,1)}), bf16[768,768]{1,0:T(8,128)(2,1)}) %all-gather.21.cloned.1.call-update) | async-done | bytes 1179664 | tf_op jit(solution)/shard_map/while/body/eval_jaxpr/all_gather | solution.py:40
  313.9 63.2 %all-gather.29.cloned.1.call-done = bf16[3072,768]{1,0:T(8,128)(2,1)} async-done(((bf16[96,768]{1,0:T(8,128)(2,1)}), bf16[3072,768]{1,0:T(8,128)(2,1)}) %all-gather.29.cloned.1.call-update) | async-done | bytes 4718608 | tf_op jit(solution)/shard_map/while/body/eval_jaxpr/all_gather | solution.py:51
  377.1 64.7 %all-gather.31.cloned.1.call-done = bf16[768,3072]{1,0:T(8,128)(2,1)} async-done(((bf16[24,3072]{1,0:T(8,128)(2,1)}), bf16[768,3072]{1,0:T(8,128)(2,1)}) %all-gather.31.cloned.1.call-update) | async-done | bytes 4718608 | tf_op jit(solution)/shard_map/while/body/eval_jaxpr/all_gather | solution.py:49
  513.7 52.9 %all-gather.17.cloned.1.call-done = bf16[768,768]{1,0:T(8,128)(2,1)} async-done(((bf16[24,768]{1,0:T(8,128)(2,1)}), bf16[768,768]{1,0:T(8,128)(2,1)}) %all-gather.17.cloned.1.call-update) | async-done | bytes 1179664 | tf_op jit(solution)/shard_map/while/body/eval_jaxpr/all_gather | solution.py:43
  574.6 47.8 %all-gather.21.cloned.1.call-done = bf16[768,768]{1,0:T(8,128)(2,1)} async-done(((bf16[24,768]{1,0:T(8,128)(2,1)}), bf16[768,768]{1,0:T(8,128)(2,1)}) %all-gather.21.cloned.1.call-update) | async-done | bytes 1179664 | tf_op jit(solution)/shard_map/while/body/eval_jaxpr/all_gather | solution.py:40
  756.1 63.1 %all-gather.29.cloned.1.call-done = bf16[3072,768]{1,0:T(8,128)(2,1)} async-done(((bf16[96,768]{1,0:T(8,128)(2,1)}), bf16[3072,768]{1,0:T(8,128)(2,1)}) %all-gather.29.cloned.1.call-update) | async-done | bytes 4718608 | tf_op jit(solution)/shard_map/while/body/eval_jaxpr/all_gather | solution.py:51
  819.2 64.6 %all-gather.31.cloned.1.call-done = bf16[768,3072]{1,0:T(8,128)(2,1)} async-done(((bf16[24,3072]{1,0:T(8,128)(2,1)}), bf16[768,3072]{1,0:T(8,128)(2,1)}) %all-gather.31.cloned.1.call-update) | async-done | bytes 4718608 | tf_op jit(solution)/shard_map/while/body/eval_jaxpr/all_gather | solution.py:49
  897.8 1116.4 %while.52 = (s32[]{:T(128)}, f32[768]{0:T(1024)}, f32[768]{0:T(1024)}, f32[768,768]{1,0:T(8,128)}, f32[768]{0:T(1024)}, /*index=5*/f32[768,768]{1,0:T(8,128)}, f...) while((s32[]{:T(128)}, f32[768]{0:T(1024)}, ...), condition=%wide.region_31.32_spmd.clone, body=%wide.region_8.31_spmd.clone.sunk | while | flops 12278196224 | bytes 516163296 | solution.py:323
  980.1 52.9 %all-gather.33.cloned.1.call-done = bf16[768,768]{1,0:T(8,128)(2,1)} async-done(((bf16[24,768]{1,0:T(8,128)(2,1)}), bf16[768,768]{1,0:T(8,128)(2,1)}) %all-gather.33.cloned.1.call-update) | async-done | bytes 1179664 | tf_op jit(solution)/shard_map/while/body/eval_jaxpr/all_gather | solution.py:42
  1039.0 49.7 %all-gather.37.cloned.1.call-done = bf16[768,768]{1,0:T(8,128)(2,1)} async-done(((bf16[24,768]{1,0:T(8,128)(2,1)}), bf16[768,768]{1,0:T(8,128)(2,1)}) %all-gather.37.cloned.1.call-update) | async-done | bytes 1179664 | tf_op jit(solution)/shard_map/while/body/eval_jaxpr/all_gather | solution.py:40
  1221.4 63.2 %all-gather.45.cloned.1.call-done = bf16[768,3072]{1,0:T(8,128)(2,1)} async-done(((bf16[24,3072]{1,0:T(8,128)(2,1)}), bf16[768,3072]{1,0:T(8,128)(2,1)}) %all-gather.45.cloned.1.call-update) | async-done | bytes 4718608 | tf_op jit(solution)/shard_map/while/body/eval_jaxpr/all_gather | solution.py:49
  1290.1 59.1 %all-gather.47.cloned.1.call-done = bf16[3072,768]{1,0:T(8,128)(2,1)} async-done(((bf16[96,768]{1,0:T(8,128)(2,1)}), bf16[3072,768]{1,0:T(8,128)(2,1)}) %all-gather.47.cloned.1.call-update) | async-done | bytes 4718608 | tf_op jit(solution)/shard_map/while/body/eval_jaxpr/all_gather | solution.py:51
  1526.7 53.0 %all-gather.33.cloned.1.call-done = bf16[768,768]{1,0:T(8,128)(2,1)} async-done(((bf16[24,768]{1,0:T(8,128)(2,1)}), bf16[768,768]{1,0:T(8,128)(2,1)}) %all-gather.33.cloned.1.call-update) | async-done | bytes 1179664 | tf_op jit(solution)/shard_map/while/body/eval_jaxpr/all_gather | solution.py:42
  1585.7 49.7 %all-gather.37.cloned.1.call-done = bf16[768,768]{1,0:T(8,128)(2,1)} async-done(((bf16[24,768]{1,0:T(8,128)(2,1)}), bf16[768,768]{1,0:T(8,128)(2,1)}) %all-gather.37.cloned.1.call-update) | async-done | bytes 1179664 | tf_op jit(solution)/shard_map/while/body/eval_jaxpr/all_gather | solution.py:40
  1768.1 63.1 %all-gather.45.cloned.1.call-done = bf16[768,3072]{1,0:T(8,128)(2,1)} async-done(((bf16[24,3072]{1,0:T(8,128)(2,1)}), bf16[768,3072]{1,0:T(8,128)(2,1)}) %all-gather.45.cloned.1.call-update) | async-done | bytes 4718608 | tf_op jit(solution)/shard_map/while/body/eval_jaxpr/all_gather | solution.py:49
  1836.7 59.3 %all-gather.47.cloned.1.call-done = bf16[3072,768]{1,0:T(8,128)(2,1)} async-done(((bf16[96,768]{1,0:T(8,128)(2,1)}), bf16[3072,768]{1,0:T(8,128)(2,1)}) %all-gather.47.cloned.1.call-update) | async-done | bytes 4718608 | tf_op jit(solution)/shard_map/while/body/eval_jaxpr/all_gather | solution.py:51
  2063.5 55.5 %reduce-scatter.9.cloned.1.call-done = f32[24,768]{1,0:T(8,128)} async-done(((f32[768,768]{1,0:T(8,128)}), f32[24,768]{1,0:T(8,128)}) %reduce-scatter.9.cloned.1.call-update) | async-done | bytes 73744 | tf_op jit(solution)/shard_map/reduce_scatter | solution.py:324
  2119.1 104.4 %reduce-scatter.11.cloned.1.call-done = f32[24,768]{1,0:T(8,128)} async-done(((f32[768,768]{1,0:T(8,128)}), f32[24,768]{1,0:T(8,128)}) %reduce-scatter.11.cloned.1.call-update) | async-done | bytes 73744 | tf_op jit(solution)/shard_map/reduce_scatter | solution.py:324
  2223.5 104.3 %reduce-scatter.13.cloned.1.call-done = f32[24,768]{1,0:T(8,128)} async-done(((f32[768,768]{1,0:T(8,128)}), f32[24,768]{1,0:T(8,128)}) %reduce-scatter.13.cloned.1.call-update) | async-done | bytes 73744 | tf_op jit(solution)/shard_map/reduce_scatter | solution.py:324
  2327.8 104.5 %reduce-scatter.15.cloned.1.call-done = f32[24,768]{1,0:T(8,128)} async-done(((f32[768,768]{1,0:T(8,128)}), f32[24,768]{1,0:T(8,128)}) %reduce-scatter.15.cloned.1.call-update) | async-done | bytes 73744 | tf_op jit(solution)/shard_map/reduce_scatter | solution.py:324
  2432.3 141.7 %reduce-scatter.17.cloned.1.call-done = f32[24,3072]{1,0:T(8,128)} async-done(((f32[768,3072]{1,0:T(8,128)}), f32[24,3072]{1,0:T(8,128)}) %reduce-scatter.17.cloned.1.call-update) | async-done | bytes 294928 | tf_op jit(solution)/shard_map/reduce_scatter | solution.py:324
  2574.0 141.7 %reduce-scatter.19.cloned.1.call-done = f32[96,768]{1,0:T(8,128)} async-done(((f32[3072,768]{1,0:T(8,128)}), f32[96,768]{1,0:T(8,128)}) %reduce-scatter.19.cloned.1.call-update) | async-done | bytes 294928 | tf_op jit(solution)/shard_map/reduce_scatter | solution.py:324
  (647 shorter events, 1122.4 us)
Async XLA Ops:
  10.5 207.8 %all-gather.25.cloned.1.call-start = ((), (), s32[]{:S(2)}) async-start(), calls=%async_computation.18 | async-start | bytes 1966080 | tf_op jit(solution)/shard_map/while/body/eval_jaxpr/all_gather | solution.py:89
  71.6 184.6 %all-gather.19.cloned.1.call-start = ((), (), s32[]{:S(2)}) async-start(), calls=%async_computation.15 | async-start | bytes 1966080 | tf_op jit(solution)/shard_map/while/body/eval_jaxpr/all_gather | solution.py:90
  127.2 184.6 %all-gather.27.cloned.1.call-start = ((), (), s32[]{:S(2)}) async-start(), calls=%async_computation.19 | async-start | bytes 1216512 | tf_op jit(solution)/shard_map/while/body/eval_jaxpr/all_gather | solution.py:45
  127.8 249.4 %all-gather.29.cloned.1.call-start = ((), (), s32[]{:S(2)}) async-start(), calls=%async_computation.20 | async-start | bytes 4866048 | tf_op jit(solution)/shard_map/while/body/eval_jaxpr/all_gather | solution.py:51
  128.5 313.3 %all-gather.31.cloned.1.call-start = ((), (), s32[]{:S(2)}) async-start(), calls=%async_computation.21 | async-start | bytes 4866048 | tf_op jit(solution)/shard_map/while/body/eval_jaxpr/all_gather | solution.py:49
  456.8 203.5 %all-gather.25.cloned.1.call-start = ((), (), s32[]{:S(2)}) async-start(), calls=%async_computation.18 | async-start | bytes 1966080 | tf_op jit(solution)/shard_map/while/body/eval_jaxpr/all_gather | solution.py:89
  513.7 184.7 %all-gather.19.cloned.1.call-start = ((), (), s32[]{:S(2)}) async-start(), calls=%async_computation.15 | async-start | bytes 1966080 | tf_op jit(solution)/shard_map/while/body/eval_jaxpr/all_gather | solution.py:90
  569.2 184.7 %all-gather.27.cloned.1.call-start = ((), (), s32[]{:S(2)}) async-start(), calls=%async_computation.19 | async-start | bytes 1216512 | tf_op jit(solution)/shard_map/while/body/eval_jaxpr/all_gather | solution.py:45
  569.8 249.4 %all-gather.29.cloned.1.call-start = ((), (), s32[]{:S(2)}) async-start(), calls=%async_computation.20 | async-start | bytes 4866048 | tf_op jit(solution)/shard_map/while/body/eval_jaxpr/all_gather | solution.py:51
  570.4 313.4 %all-gather.31.cloned.1.call-start = ((), (), s32[]{:S(2)}) async-start(), calls=%async_computation.21 | async-start | bytes 4866048 | tf_op jit(solution)/shard_map/while/body/eval_jaxpr/all_gather | solution.py:49
  923.3 202.8 %all-gather.41.cloned.1.call-start = ((), (), s32[]{:S(2)}) async-start(), calls=%async_computation.26 | async-start | bytes 1966080 | tf_op jit(solution)/shard_map/while/body/eval_jaxpr/all_gather | solution.py:90
  1036.3 248.3 %all-gather.45.cloned.1.call-start = ((), (), s32[]{:S(2)}) async-start(), calls=%async_computation.28 | async-start | bytes 4866048 | tf_op jit(solution)/shard_map/while/body/eval_jaxpr/all_gather | solution.py:49
  1037.0 312.2 %all-gather.47.cloned.1.call-start = ((), (), s32[]{:S(2)}) async-start(), calls=%async_computation.29 | async-start | bytes 4866048 | tf_op jit(solution)/shard_map/while/body/eval_jaxpr/all_gather | solution.py:51
  1037.6 391.2 %reduce-scatter.21.cloned.1.call-start = ((), (), s32[]{:S(2)}) async-start(), calls=%async_computation.30 | async-start | bytes 1966080 | tf_op jit(solution)/shard_map/while/body/eval_jaxpr/reduce_scatter | solution.py:214
  1469.6 203.2 %all-gather.41.cloned.1.call-start = ((), (), s32[]{:S(2)}) async-start(), calls=%async_computation.26 | async-start | bytes 1966080 | tf_op jit(solution)/shard_map/while/body/eval_jaxpr/all_gather | solution.py:90
  1582.3 183.7 %all-gather.43.cloned.1.call-start = ((), (), s32[]{:S(2)}) async-start(), calls=%async_computation.27 | async-start | bytes 1216512 | tf_op jit(solution)/shard_map/while/body/eval_jaxpr/all_gather | solution.py:45
  1583.0 248.2 %all-gather.45.cloned.1.call-start = ((), (), s32[]{:S(2)}) async-start(), calls=%async_computation.28 | async-start | bytes 4866048 | tf_op jit(solution)/shard_map/while/body/eval_jaxpr/all_gather | solution.py:49
  1583.6 312.3 %all-gather.47.cloned.1.call-start = ((), (), s32[]{:S(2)}) async-start(), calls=%async_computation.29 | async-start | bytes 4866048 | tf_op jit(solution)/shard_map/while/body/eval_jaxpr/all_gather | solution.py:51
  1584.3 398.7 %reduce-scatter.21.cloned.1.call-start = ((), (), s32[]{:S(2)}) async-start(), calls=%async_computation.30 | async-start | bytes 1966080 | tf_op jit(solution)/shard_map/while/body/eval_jaxpr/reduce_scatter | solution.py:214
  2014.8 208.7 %reduce-scatter.11.cloned.1.call-start = ((), (), s32[]{:S(2)}) async-start(), calls=%async_computation.9 | async-start | bytes 2433024 | tf_op jit(solution)/shard_map/reduce_scatter | solution.py:324
  2015.4 312.4 %reduce-scatter.13.cloned.1.call-start = ((), (), s32[]{:S(2)}) async-start(), calls=%async_computation.10 | async-start | bytes 2433024 | tf_op jit(solution)/shard_map/reduce_scatter | solution.py:324
  2015.9 416.3 %reduce-scatter.15.cloned.1.call-start = ((), (), s32[]{:S(2)}) async-start(), calls=%async_computation.11 | async-start | bytes 2433024 | tf_op jit(solution)/shard_map/reduce_scatter | solution.py:324
  2016.7 557.3 %reduce-scatter.17.cloned.1.call-start = ((), (), s32[]{:S(2)}) async-start(), calls=%async_computation.12 | async-start | bytes 9732096 | tf_op jit(solution)/shard_map/reduce_scatter | solution.py:324
  2017.4 698.3 %reduce-scatter.19.cloned.1.call-start = ((), (), s32[]{:S(2)}) async-start(), calls=%async_computation.13 | async-start | bytes 9732096 | tf_op jit(solution)/shard_map/reduce_scatter | solution.py:324
  (150 other events, 5973.7 us)
Sparse Core Ops, SparseCore 0:
  11.9 56.9 all-gather.22
  71.7 52.8 all-gather.16
  127.4 52.9 all-gather.20
  258.9 52.8 all-gather.26
  314.6 62.5 all-gather.28
  379.9 61.8 all-gather.30
  458.4 52.5 all-gather.22
  513.6 52.9 all-gather.16
  569.4 52.9 all-gather.20
  701.1 52.8 all-gather.26
  756.6 62.5 all-gather.28
  821.8 61.8 all-gather.30
  924.7 52.6 all-gather.38
  980.0 52.9 all-gather.32
  1035.7 52.8 all-gather.36
  1166.4 52.8 all-gather.42
  1222.1 62.5 all-gather.44
  1287.3 61.8 all-gather.46
  1470.8 53.0 all-gather.38
  1526.7 52.8 all-gather.32
  1582.5 52.9 all-gather.36
  1713.1 52.8 all-gather.42
  1768.7 62.5 all-gather.44
  1834.0 61.8 all-gather.46
  (12 shorter events, 422.8 us)
Sparse Core Ops, SparseCore 1:
  2020.5 98.5 reduce-scatter.8
  2124.8 98.6 reduce-scatter.10
  2229.2 98.5 reduce-scatter.12
  2333.7 98.5 reduce-scatter.14
  2438.8 135.2 reduce-scatter.16
  2580.5 135.2 reduce-scatter.18
where the time goes:
time: 2740 us; the launch traced here: 2720 us
  waiting for transfers between devices  2090 us (76%)
  matrix products  274 us (10%)
  blocking collectives  201 us (7%)
  local copies, waits for them, and re-layouts  77.8 us (3%)
  other arithmetic  38.4 us (1%)
    reduce_scatter x6, waiting for transfers between devices, per_device(): lax.psum_scatter(totals, ('dp', 'ctx'), scatter_dimension=0, tiled=True)  652 us
    all_gather x4, waiting for transfers between devices, fetch(): lax.all_gather(shards[11], ('dp', 'ctx'), axis=0, tiled=True)  256 us
    all_gather x4, waiting for transfers between devices, fetch(): lax.all_gather(shards[13], ('dp', 'ctx'), axis=0, tiled=True)  245 us
    all_gather x4, waiting for transfers between devices, fetch(): lax.all_gather(shards[2], ('dp', 'ctx'), axis=0, tiled=True)  195 us
    while x4, blocking collectives  161 us
    all_gather x4, waiting for transfers between devices, fetch(): lax.all_gather(shards[7], ('dp', 'ctx'), axis=0, tiled=True)  155 us
    all_gather x4, waiting for transfers between devices, forward(): lax.all_gather(value_rows, 'ctx', axis=0, tiled=True)  143 us
    all_gather x4, waiting for transfers between devices, forward(): lax.all_gather(key_rows, 'ctx', axis=0, tiled=True)  142 us
  transfers between devices with their start and end apart: 42, of which 40 were waited for; matrix products, arithmetic and copies ran while one was open for 10% of the time, Pallas kernels for 0%

commit v1 on v0

--- a/solution.py
+++ b/solution.py
@@ -7,6 +7,18 @@
 HD = 64
 
 
+def gather_by_bits(x, axis, dim):
+    ways, here, step = (lax.axis_size(axis), lax.axis_index(axis), x.shape[dim])
+    line, have = (x, 1)
+    while have < ways:
+        line = jnp.concatenate(
+            [line, lax.ppermute(line, axis, [(d, (d - have) % ways) for d in range(ways)])],
+            axis=dim,
+        )
+        have = 2 * have
+    return jnp.roll(line, here * step, axis=dim)
+
+
 def layer_norm(tok_rows, gain, shift):
     center = tok_rows - jnp.mean(tok_rows, axis=-1, keepdims=True)
     spread = jnp.mean(center * center, axis=-1, keepdims=True)
@@ -37,7 +49,7 @@
     return (
         lax.all_gather(shards[0], ("dp", "ctx"), axis=0, tiled=True),
         lax.all_gather(shards[1], ("dp", "ctx"), axis=0, tiled=True),
-        lax.all_gather(shards[2], ("dp", "ctx"), axis=0, tiled=True),
+        gather_by_bits(shards[2], ("dp", "ctx"), 0),
         lax.all_gather(shards[3], ("dp", "ctx"), axis=0, tiled=True),
         lax.all_gather(shards[4], ("dp", "ctx"), axis=0, tiled=True),
         lax.all_gather(shards[5], ("dp", "ctx"), axis=0, tiled=True),

time: 2740 us -> 2560 us (0.934)
  waiting for transfers between devices: 2090 us -> 1910 us
    all_gather x4 -> x0, waiting for transfers between devices: 195 us -> none  [fetch(): lax.all_gather(shards[2], ('dp', 'ctx'), axis=0, tiled=True)]
    ppermute x0 -> x5, waiting for transfers between devices: none -> 30.7 us  [gather_by_bits(): lax.ppermute(line, axis, [(d, (d - have) % ways) for d in range(ways)])]
  transfers between devices with their start and end apart: 42 -> 43, of which waited for: 40 -> 41; matrix products, arithmetic and copies ran while one was open for 10% -> 10% of each run, Pallas kernels for 0% -> 0%
where the time goes in v1:
time: 2560 us; the launch traced here: 2550 us
  waiting for transfers between devices  1910 us (75%)
  matrix products  277 us (11%)
  blocking collectives  200 us (8%)
  local copies, waits for them, and re-layouts  80 us (3%)
  other arithmetic  32.2 us (1%)
  loops' own time  27.6 us (1%)
    reduce_scatter x6, waiting for transfers between devices, per_device(): lax.psum_scatter(totals, ('dp', 'ctx'), scatter_dimension=0, tiled=True)  652 us
    all_gather x4, waiting for transfers between devices, fetch(): lax.all_gather(shards[11], ('dp', 'ctx'), axis=0, tiled=True)  256 us
    all_gather x4, waiting for transfers between devices, fetch(): lax.all_gather(shards[13], ('dp', 'ctx'), axis=0, tiled=True)  245 us
    while x4, blocking collectives  160 us
    all_gather x4, waiting for transfers between devices, fetch(): lax.all_gather(shards[7], ('dp', 'ctx'), axis=0, tiled=True)  154 us
    all_gather x4, waiting for transfers between devices, forward(): lax.all_gather(value_rows, 'ctx', axis=0, tiled=True)  128 us
    all_gather x4, waiting for transfers between devices, fetch(): lax.all_gather(shards[4], ('dp', 'ctx'), axis=0, tiled=True)  123 us
    all_gather x4, waiting for transfers between devices, forward(): lax.all_gather(key_rows, 'ctx', axis=0, tiled=True)  123 us
  transfers between devices with their start and end apart: 43, of which 41 were waited for; matrix products, arithmetic and copies ran while one was open for 10% of the time, Pallas kernels for 0%

profile of v1, /device:TPU:0, one launch (start us, length us, event | category | flops | bytes accessed | tf_op | source)
XLA Modules:
  0.0 2547.6 jit_solution(16398912482839072735)
XLA Ops:
  54.3 776.4 %while.55 = (s32[]{:T(128)}, bf16[2,256,768]{2,1,0:T(8,128)(2,1)S(1)}, bf16[2,256,768]{2,1,0:T(8,128)(2,1)S(1)}, bf16[24]{0:T(256)(128)(2,1)}, bf16[24]{0:T(256)...) while((s32[]{:T(128)}, ...), condition=%wide.region_7.9_spmd, body=%wide.region_0.8_spmd.sunk | while | flops 4511191552 | bytes 110000456 | solution.py:319
  62.7 41.3 %all-reduce.39 = (bf16[768]{0:T(1024)(128)(2,1)S(1)}, bf16[768]{0:T(1024)(128)(2,1)S(1)}, bf16[768]{0:T(1024)(128)(2,1)S(1)}, bf16[768]{0:T(1024)(128)(2,1)S(1)}...) all-reduce(bf16[768]{0:T(1024)(128)(2,1)S(1)} %dynamic-update-slice, ...), channel_id=1, replica_groups=mesh['dp'=8,'ctx'=4] {'dp','ctx'}, use_global_device_ids=true, to_apply=%add.2 | all-reduce | flops 9216 | bytes 36864 | tf_op jit(solution)/shard_map/while
  116.5 53.3 %all-gather.15.cloned.1.call-done = bf16[768,768]{1,0:T(8,128)(2,1)} async-done(((bf16[24,768]{1,0:T(8,128)(2,1)}), bf16[768,768]{1,0:T(8,128)(2,1)}) %all-gather.15.cloned.1.call-update) | async-done | bytes 1179664 | tf_op jit(solution)/shard_map/while/body/eval_jaxpr/all_gather | solution.py:55
  303.5 63.1 %all-gather.25.cloned.1.call-done = bf16[3072,768]{1,0:T(8,128)(2,1)} async-done(((bf16[96,768]{1,0:T(8,128)(2,1)}), bf16[3072,768]{1,0:T(8,128)(2,1)}) %all-gather.25.cloned.1.call-update) | async-done | bytes 4718608 | tf_op jit(solution)/shard_map/while/body/eval_jaxpr/all_gather | solution.py:63
  366.6 64.7 %all-gather.27.cloned.1.call-done = bf16[768,3072]{1,0:T(8,128)(2,1)} async-done(((bf16[24,3072]{1,0:T(8,128)(2,1)}), bf16[768,3072]{1,0:T(8,128)(2,1)}) %all-gather.27.cloned.1.call-update) | async-done | bytes 4718608 | tf_op jit(solution)/shard_map/while/body/eval_jaxpr/all_gather | solution.py:61
  452.8 39.9 %all-reduce.39 = (bf16[768]{0:T(1024)(128)(2,1)S(1)}, bf16[768]{0:T(1024)(128)(2,1)S(1)}, bf16[768]{0:T(1024)(128)(2,1)S(1)}, bf16[768]{0:T(1024)(128)(2,1)S(1)}...) all-reduce(bf16[768]{0:T(1024)(128)(2,1)S(1)} %dynamic-update-slice, ...), channel_id=1, replica_groups=mesh['dp'=8,'ctx'=4] {'dp','ctx'}, use_global_device_ids=true, to_apply=%add.2 | all-reduce | flops 9216 | bytes 36864 | tf_op jit(solution)/shard_map/while
  503.2 53.0 %all-gather.15.cloned.1.call-done = bf16[768,768]{1,0:T(8,128)(2,1)} async-done(((bf16[24,768]{1,0:T(8,128)(2,1)}), bf16[768,768]{1,0:T(8,128)(2,1)}) %all-gather.15.cloned.1.call-update) | async-done | bytes 1179664 | tf_op jit(solution)/shard_map/while/body/eval_jaxpr/all_gather | solution.py:55
  689.9 63.2 %all-gather.25.cloned.1.call-done = bf16[3072,768]{1,0:T(8,128)(2,1)} async-done(((bf16[96,768]{1,0:T(8,128)(2,1)}), bf16[3072,768]{1,0:T(8,128)(2,1)}) %all-gather.25.cloned.1.call-update) | async-done | bytes 4718608 | tf_op jit(solution)/shard_map/while/body/eval_jaxpr/all_gather | solution.py:63
  753.2 64.6 %all-gather.27.cloned.1.call-done = bf16[768,3072]{1,0:T(8,128)(2,1)} async-done(((bf16[24,3072]{1,0:T(8,128)(2,1)}), bf16[768,3072]{1,0:T(8,128)(2,1)}) %all-gather.27.cloned.1.call-update) | async-done | bytes 4718608 | tf_op jit(solution)/shard_map/while/body/eval_jaxpr/all_gather | solution.py:61
  831.8 1006.9 %while.56 = (s32[]{:T(128)}, f32[768]{0:T(1024)}, f32[768]{0:T(1024)}, f32[768,768]{1,0:T(8,128)}, f32[768]{0:T(1024)}, /*index=5*/f32[768,768]{1,0:T(8,128)}, f...) while((s32[]{:T(128)}, f32[768]{0:T(1024)}, ...), condition=%wide.region_31.33_spmd.clone, body=%wide.region_8.32_spmd.clone.sunk | while | flops 12282914816 | bytes 534598752 | solution.py:335
  913.0 53.1 %all-gather.29.cloned.1.call-done = bf16[768,768]{1,0:T(8,128)(2,1)} async-done(((bf16[24,768]{1,0:T(8,128)(2,1)}), bf16[768,768]{1,0:T(8,128)(2,1)}) %all-gather.29.cloned.1.call-update) | async-done | bytes 1179664 | tf_op jit(solution)/shard_map/while/body/eval_jaxpr/all_gather | solution.py:54
  1056.8 39.7 %all-gather.37.cloned.1.call-done = bf16[768,768]{1,0:T(8,128)(2,1)} async-done(((bf16[24,768]{1,0:T(8,128)(2,1)}), bf16[768,768]{1,0:T(8,128)(2,1)}) %all-gather.37.cloned.1.call-update) | async-done | bytes 1179664 | tf_op jit(solution)/shard_map/while/body/eval_jaxpr/all_gather | solution.py:57
  1098.6 63.1 %all-gather.39.cloned.1.call-done = bf16[768,3072]{1,0:T(8,128)(2,1)} async-done(((bf16[24,3072]{1,0:T(8,128)(2,1)}), bf16[768,3072]{1,0:T(8,128)(2,1)}) %all-gather.39.cloned.1.call-update) | async-done | bytes 4718608 | tf_op jit(solution)/shard_map/while/body/eval_jaxpr/all_gather | solution.py:61
  1167.2 59.2 %all-gather.41.cloned.1.call-done = bf16[3072,768]{1,0:T(8,128)(2,1)} async-done(((bf16[96,768]{1,0:T(8,128)(2,1)}), bf16[3072,768]{1,0:T(8,128)(2,1)}) %all-gather.41.cloned.1.call-update) | async-done | bytes 4718608 | tf_op jit(solution)/shard_map/while/body/eval_jaxpr/all_gather | solution.py:63
  1404.4 52.9 %all-gather.29.cloned.1.call-done = bf16[768,768]{1,0:T(8,128)(2,1)} async-done(((bf16[24,768]{1,0:T(8,128)(2,1)}), bf16[768,768]{1,0:T(8,128)(2,1)}) %all-gather.29.cloned.1.call-update) | async-done | bytes 1179664 | tf_op jit(solution)/shard_map/while/body/eval_jaxpr/all_gather | solution.py:54
  1589.8 63.2 %all-gather.39.cloned.1.call-done = bf16[768,3072]{1,0:T(8,128)(2,1)} async-done(((bf16[24,3072]{1,0:T(8,128)(2,1)}), bf16[768,3072]{1,0:T(8,128)(2,1)}) %all-gather.39.cloned.1.call-update) | async-done | bytes 4718608 | tf_op jit(solution)/shard_map/while/body/eval_jaxpr/all_gather | solution.py:61
  1658.6 59.1 %all-gather.41.cloned.1.call-done = bf16[3072,768]{1,0:T(8,128)(2,1)} async-done(((bf16[96,768]{1,0:T(8,128)(2,1)}), bf16[3072,768]{1,0:T(8,128)(2,1)}) %all-gather.41.cloned.1.call-update) | async-done | bytes 4718608 | tf_op jit(solution)/shard_map/while/body/eval_jaxpr/all_gather | solution.py:63
  1842.8 39.9 %all-reduce.36 = (f32[768]{0:T(1024)S(1)}, f32[768]{0:T(1024)S(1)}, f32[768]{0:T(1024)S(1)}, f32[768]{0:T(1024)S(1)}, f32[768]{0:T(1024)S(1)}, /*index=5*/f32[76...) all-reduce(f32[768]{0:T(1024)S(1)} %copy-done.64, ...), channel_id=4, replica_groups=mesh['dp'=8,'ctx'=4] {'dp','ctx'}, use_global_device_ids=true, to_apply=%region_32.34.clone | all-reduce | flops 9216 | bytes 73728
  1888.0 55.5 %reduce-scatter.9.cloned.1.call-done = f32[24,768]{1,0:T(8,128)} async-done(((f32[768,768]{1,0:T(8,128)}), f32[24,768]{1,0:T(8,128)}) %reduce-scatter.9.cloned.1.call-update) | async-done | bytes 73744 | tf_op jit(solution)/shard_map/reduce_scatter | solution.py:336
  1943.5 104.4 %reduce-scatter.11.cloned.1.call-done = f32[24,768]{1,0:T(8,128)} async-done(((f32[768,768]{1,0:T(8,128)}), f32[24,768]{1,0:T(8,128)}) %reduce-scatter.11.cloned.1.call-update) | async-done | bytes 73744 | tf_op jit(solution)/shard_map/reduce_scatter | solution.py:336
  2047.9 104.4 %reduce-scatter.13.cloned.1.call-done = f32[24,768]{1,0:T(8,128)} async-done(((f32[768,768]{1,0:T(8,128)}), f32[24,768]{1,0:T(8,128)}) %reduce-scatter.13.cloned.1.call-update) | async-done | bytes 73744 | tf_op jit(solution)/shard_map/reduce_scatter | solution.py:336
  2152.2 104.5 %reduce-scatter.15.cloned.1.call-done = f32[24,768]{1,0:T(8,128)} async-done(((f32[768,768]{1,0:T(8,128)}), f32[24,768]{1,0:T(8,128)}) %reduce-scatter.15.cloned.1.call-update) | async-done | bytes 73744 | tf_op jit(solution)/shard_map/reduce_scatter | solution.py:336
  2256.7 141.8 %reduce-scatter.17.cloned.1.call-done = f32[24,3072]{1,0:T(8,128)} async-done(((f32[768,3072]{1,0:T(8,128)}), f32[24,3072]{1,0:T(8,128)}) %reduce-scatter.17.cloned.1.call-update) | async-done | bytes 294928 | tf_op jit(solution)/shard_map/reduce_scatter | solution.py:336
  2398.5 141.7 %reduce-scatter.19.cloned.1.call-done = f32[96,768]{1,0:T(8,128)} async-done(((f32[3072,768]{1,0:T(8,128)}), f32[96,768]{1,0:T(8,128)}) %reduce-scatter.19.cloned.1.call-update) | async-done | bytes 294928 | tf_op jit(solution)/shard_map/reduce_scatter | solution.py:336
  (688 shorter events, 978.6 us)
Async XLA Ops:
  55.8 152.2 %all-gather.21.cloned.1.call-start = ((), (), s32[]{:S(2)}) async-start(), calls=%async_computation.17 | async-start | bytes 1966080 | tf_op jit(solution)/shard_map/while/body/eval_jaxpr/all_gather | solution.py:101
  116.4 129.5 %all-gather.17.cloned.1.call-start = ((), (), s32[]{:S(2)}) async-start(), calls=%async_computation.15 | async-start | bytes 1966080 | tf_op jit(solution)/shard_map/while/body/eval_jaxpr/all_gather | solution.py:102
  172.4 129.0 %all-gather.23.cloned.1.call-start = ((), (), s32[]{:S(2)}) async-start(), calls=%async_computation.18 | async-start | bytes 1216512 | tf_op jit(solution)/shard_map/while/body/eval_jaxpr/all_gather | solution.py:57
  173.0 193.6 %all-gather.25.cloned.1.call-start = ((), (), s32[]{:S(2)}) async-start(), calls=%async_computation.19 | async-start | bytes 4866048 | tf_op jit(solution)/shard_map/while/body/eval_jaxpr/all_gather | solution.py:63
  173.6 257.8 %all-gather.27.cloned.1.call-start = ((), (), s32[]{:S(2)}) async-start(), calls=%async_computation.20 | async-start | bytes 4866048 | tf_op jit(solution)/shard_map/while/body/eval_jaxpr/all_gather | solution.py:61
  445.8 148.5 %all-gather.21.cloned.1.call-start = ((), (), s32[]{:S(2)}) async-start(), calls=%async_computation.17 | async-start | bytes 1966080 | tf_op jit(solution)/shard_map/while/body/eval_jaxpr/all_gather | solution.py:101
  503.2 129.1 %all-gather.17.cloned.1.call-start = ((), (), s32[]{:S(2)}) async-start(), calls=%async_computation.15 | async-start | bytes 1966080 | tf_op jit(solution)/shard_map/while/body/eval_jaxpr/all_gather | solution.py:102
  558.8 129.0 %all-gather.23.cloned.1.call-start = ((), (), s32[]{:S(2)}) async-start(), calls=%async_computation.18 | async-start | bytes 1216512 | tf_op jit(solution)/shard_map/while/body/eval_jaxpr/all_gather | solution.py:57
  559.4 193.8 %all-gather.25.cloned.1.call-start = ((), (), s32[]{:S(2)}) async-start(), calls=%async_computation.19 | async-start | bytes 4866048 | tf_op jit(solution)/shard_map/while/body/eval_jaxpr/all_gather | solution.py:63
  560.2 257.6 %all-gather.27.cloned.1.call-start = ((), (), s32[]{:S(2)}) async-start(), calls=%async_computation.20 | async-start | bytes 4866048 | tf_op jit(solution)/shard_map/while/body/eval_jaxpr/all_gather | solution.py:61
  855.7 147.7 %all-gather.35.cloned.1.call-start = ((), (), s32[]{:S(2)}) async-start(), calls=%async_computation.24 | async-start | bytes 1966080 | tf_op jit(solution)/shard_map/while/body/eval_jaxpr/all_gather | solution.py:102
  912.9 127.9 %all-gather.31.cloned.1.call-start = ((), (), s32[]{:S(2)}) async-start(), calls=%async_computation.22 | async-start | bytes 1966080 | tf_op jit(solution)/shard_map/while/body/eval_jaxpr/all_gather | solution.py:101
  969.4 192.3 %all-gather.39.cloned.1.call-start = ((), (), s32[]{:S(2)}) async-start(), calls=%async_computation.26 | async-start | bytes 4866048 | tf_op jit(solution)/shard_map/while/body/eval_jaxpr/all_gather | solution.py:61
  970.0 256.4 %all-gather.41.cloned.1.call-start = ((), (), s32[]{:S(2)}) async-start(), calls=%async_computation.27 | async-start | bytes 4866048 | tf_op jit(solution)/shard_map/while/body/eval_jaxpr/all_gather | solution.py:63
  970.7 333.1 %reduce-scatter.21.cloned.1.call-start = ((), (), s32[]{:S(2)}) async-start(), calls=%async_computation.28 | async-start | bytes 1966080 | tf_op jit(solution)/shard_map/while/body/eval_jaxpr/reduce_scatter | solution.py:226
  1346.6 148.1 %all-gather.35.cloned.1.call-start = ((), (), s32[]{:S(2)}) async-start(), calls=%async_computation.24 | async-start | bytes 1966080 | tf_op jit(solution)/shard_map/while/body/eval_jaxpr/all_gather | solution.py:102
  1460.6 192.4 %all-gather.39.cloned.1.call-start = ((), (), s32[]{:S(2)}) async-start(), calls=%async_computation.26 | async-start | bytes 4866048 | tf_op jit(solution)/shard_map/while/body/eval_jaxpr/all_gather | solution.py:61
  1461.3 256.3 %all-gather.41.cloned.1.call-start = ((), (), s32[]{:S(2)}) async-start(), calls=%async_computation.27 | async-start | bytes 4866048 | tf_op jit(solution)/shard_map/while/body/eval_jaxpr/all_gather | solution.py:63
  1461.9 339.9 %reduce-scatter.21.cloned.1.call-start = ((), (), s32[]{:S(2)}) async-start(), calls=%async_computation.28 | async-start | bytes 1966080 | tf_op jit(solution)/shard_map/while/body/eval_jaxpr/reduce_scatter | solution.py:226
  1839.3 208.6 %reduce-scatter.11.cloned.1.call-start = ((), (), s32[]{:S(2)}) async-start(), calls=%async_computation.9 | async-start | bytes 2433024 | tf_op jit(solution)/shard_map/reduce_scatter | solution.py:336
  1839.9 312.3 %reduce-scatter.13.cloned.1.call-start = ((), (), s32[]{:S(2)}) async-start(), calls=%async_computation.10 | async-start | bytes 2433024 | tf_op jit(solution)/shard_map/reduce_scatter | solution.py:336
  1840.5 416.3 %reduce-scatter.15.cloned.1.call-start = ((), (), s32[]{:S(2)}) async-start(), calls=%async_computation.11 | async-start | bytes 2433024 | tf_op jit(solution)/shard_map/reduce_scatter | solution.py:336
  1841.2 557.3 %reduce-scatter.17.cloned.1.call-start = ((), (), s32[]{:S(2)}) async-start(), calls=%async_computation.12 | async-start | bytes 9732096 | tf_op jit(solution)/shard_map/reduce_scatter | solution.py:336
  1842.0 698.3 %reduce-scatter.19.cloned.1.call-start = ((), (), s32[]{:S(2)}) async-start(), calls=%async_computation.13 | async-start | bytes 9732096 | tf_op jit(solution)/shard_map/reduce_scatter | solution.py:336
  (167 other events, 4742.6 us)
Sparse Core Ops, SparseCore 0:
  57.9 55.9 all-gather.18
  116.7 53.1 all-gather.14
  172.0 35.9 all-gather.20
  248.5 52.8 all-gather.22
  304.1 62.5 all-gather.24
  369.4 61.8 all-gather.26
  447.9 52.6 all-gather.18
  503.4 52.8 all-gather.14
  558.2 35.9 all-gather.20
  635.0 52.8 all-gather.22
  690.6 62.5 all-gather.24
  755.8 61.8 all-gather.26
  857.8 52.4 all-gather.32
  913.0 53.0 all-gather.28
  967.4 35.9 all-gather.34
  1043.6 52.8 all-gather.36
  1099.1 62.5 all-gather.38
  1164.5 61.8 all-gather.40
  1348.6 53.1 all-gather.32
  1404.5 52.6 all-gather.28
  1458.7 35.9 all-gather.34
  1534.8 52.8 all-gather.36
  1590.5 62.5 all-gather.38
  1655.7 61.8 all-gather.40
  (8 shorter events, 279.3 us)
Sparse Core Ops, SparseCore 1:
  1845.1 98.4 reduce-scatter.8
  1949.2 98.6 reduce-scatter.10
  2053.6 98.6 reduce-scatter.12
  2158.1 98.6 reduce-scatter.14
  2263.2 135.2 reduce-scatter.16
  2405.0 135.2 reduce-scatter.18
